TPU v7x, 128 devices: a whole 4x4x4 slice. The times are simulated.
128 devices in a mesh: seq: 32 (over x, z, y_lo), dp: 4 (over y_hi, core).
Axes of the slice: x: 4, y: 4 (y_hi: 2, y_lo: 2; y = y_hi * 2 + y_lo), z: 4, core: 2. Of those that a mesh axis runs over, the one named last changes fastest.
Arguments:
- signal: bfloat16 [65536, 128], P(('seq', 'dp')), may hold values from -6 to 6
- filter_param: bfloat16 [65536, 128], P(('seq', 'dp')), may hold values from -6 to 6
- skip_gain: float32 [128], replicated, may hold values from 0.5 to 1.5
- out_grad: bfloat16 [65536, 128], P(('seq', 'dp')), may hold values from -6 to 6
Outputs:
- conv_out: bfloat16 [65536, 128], P(('seq', 'dp'))
- input_grad: bfloat16 [65536, 128], P(('seq', 'dp'))
- filter_grad: float32 [65536, 128], P(('seq', 'dp'))
All inputs are finite; a program needn't handle non-finite values.
Results may differ from a plain program's by a relative error of at most 0.001.
Values may be sent and summed in bfloat16 or wider, within the bound.
No kernel may reach another device: no remote copies, remote signals or barrier semaphores. Data moves between devices by JAX's collectives and lax.ppermute only.
A program may use at most 64 MiB of HBM per device.

v0:
```python
import math
import numpy as np
import jax
import jax.numpy as jnp
from jax import lax
from jax.sharding import PartitionSpec as P

FIRST_LEN = 512
AXES = ("seq", "dp")
highest = lax.Precision.HIGHEST


def half_table(order):
    half = order // 2
    slot = np.arange(half)[:, None]
    pos = np.arange(order)[None, :]
    angle = slot * pos % order * (2.0 * np.pi / order)
    real_rows = np.cos(angle)
    imag_rows = -np.sin(angle)
    real_rows[0, :] = 1.0
    imag_rows[0, :] = np.where(np.arange(order) % 2 == 0, 1.0, -1.0)
    return jnp.asarray(np.concatenate([real_rows, imag_rows], axis=0), dtype=jnp.float32)


def full_table(order):
    idx = np.arange(order)
    angle = idx[:, None] * idx[None, :] % order * (2.0 * np.pi / order)
    c, s = (np.cos(angle), np.sin(angle))
    top = np.concatenate([c, s], axis=1)
    bottom = np.concatenate([-s, c], axis=1)
    return jnp.asarray(np.concatenate([top, bottom], axis=0), dtype=jnp.float32)


def rotate(re, im, cos_t, sin_t):
    return (re * cos_t - im * sin_t, re * sin_t + im * cos_t)


def per_device(signal, filter_param, skip_gain, out_grad):
    dev_count = lax.axis_size(AXES)
    me = lax.axis_index(AXES)
    tok_rows, chans = signal.shape
    length = tok_rows * dev_count
    first_len = FIRST_LEN
    second_len = length // first_len
    first_dev = first_len // dev_count
    half = first_len // 2
    slots = half // dev_count
    assert second_len == dev_count and slots * dev_count == half
    stacked = jnp.concatenate([signal, out_grad, filter_param], axis=1)
    blocks = stacked.reshape(first_dev, second_len, 3 * chans)
    columns = lax.all_to_all(blocks, AXES, split_axis=1, concat_axis=0, tiled=True)
    columns = columns.reshape(first_len, 3 * chans).astype(jnp.float32)
    table_a = half_table(first_len)
    part = jnp.dot(table_a, columns, precision=highest)
    part = part.reshape(2, dev_count, slots, 3 * chans)
    got = lax.all_to_all(part, AXES, split_axis=1, concat_axis=1, tiled=True)
    z_re, z_im = (got[0], got[1])
    pos_b = jnp.arange(second_len, dtype=jnp.float32)[:, None]
    freq = (me * slots + jnp.arange(slots, dtype=jnp.int32)).astype(jnp.float32)[None, :]
    phase = pos_b * freq * (-2.0 * math.pi / length)
    tw_c = jnp.cos(phase)[:, :, None]
    tw_s = jnp.sin(phase)[:, :, None]
    t_re, t_im = rotate(z_re, z_im, tw_c, tw_s)
    is_first = me == 0
    t_im0 = jnp.where(is_first, 0.0, t_im[:, 0:1])
    nyq_phase = pos_b * (-2.0 * math.pi * half / length)
    nyq_c = jnp.cos(nyq_phase)[:, :, None]
    nyq_s = jnp.sin(nyq_phase)[:, :, None]
    extra_re = jnp.where(is_first, z_im[:, 0:1] * nyq_c, 0.0)
    extra_im = jnp.where(is_first, z_im[:, 0:1] * nyq_s, 0.0)
    rows_re = jnp.concatenate([t_re, extra_re], axis=1)
    rows_im = jnp.concatenate([t_im0, t_im[:, 1:], extra_im], axis=1)
    nrows = slots + 1
    table_b = full_table(second_len)
    both = jnp.stack([rows_re, rows_im]).reshape(2 * second_len, nrows * 3 * chans)
    spec = jnp.dot(table_b, both, precision=highest).reshape(2, second_len, nrows, 3 * chans)
    sr, si = (spec[0], spec[1])
    sig_r, cot_r, flt_r = (sr[..., :chans], sr[..., chans : 2 * chans], sr[..., 2 * chans :])
    sig_i, cot_i, flt_i = (si[..., :chans], si[..., chans : 2 * chans], si[..., 2 * chans :])
    scale = 1.0 / (math.sqrt(length) * length)
    conv_r = (sig_r * flt_r - sig_i * flt_i) * scale
    conv_i = (sig_r * flt_i + sig_i * flt_r) * scale
    back_r = (flt_r * cot_r + flt_i * cot_i) * scale
    back_i = (flt_r * cot_i - flt_i * cot_r) * scale
    taps_r = (sig_r * cot_r + sig_i * cot_i) * scale
    taps_i = (sig_r * cot_i - sig_i * cot_r) * scale
    prod = jnp.stack(
        [
            jnp.concatenate([conv_r, back_r, taps_r], axis=-1),
            jnp.concatenate([conv_i, back_i, taps_i], axis=-1),
        ]
    ).reshape(2 * second_len, nrows * 3 * chans)
    unit = lax.dot_general(table_b, prod, (((0,), (0,)), ((), ())), precision=highest).reshape(
        2, second_len, nrows, 3 * chans
    )
    u_re, u_im = (unit[0], unit[1])
    v_re, v_im = rotate(u_re[:, :slots], u_im[:, :slots], tw_c, -tw_s)
    x_re, _ = rotate(u_re[:, slots:], u_im[:, slots:], nyq_c, -nyq_s)
    out_re0 = jnp.where(is_first, v_re[:, 0:1], 2.0 * v_re[:, 0:1])
    out_im0 = jnp.where(is_first, x_re, 2.0 * v_im[:, 0:1])
    out_re = jnp.concatenate([out_re0, 2.0 * v_re[:, 1:]], axis=1)
    out_im = jnp.concatenate([out_im0, 2.0 * v_im[:, 1:]], axis=1)
    back_part = jnp.stack([out_re, out_im])
    ret = lax.all_to_all(back_part, AXES, split_axis=1, concat_axis=1, tiled=True)
    ret = ret.reshape(first_len, 3 * chans)
    times = lax.dot_general(table_a, ret, (((0,), (0,)), ((), ())), precision=highest)
    conv_cols = times[:, :chans] + skip_gain * columns[:, :chans]
    back_cols = times[:, chans : 2 * chans] + skip_gain * columns[:, chans : 2 * chans]
    taps_cols = times[:, 2 * chans :]
    taps_hi = lax.reduce_precision(taps_cols, exponent_bits=8, mantissa_bits=7)
    taps_lo = taps_cols - taps_hi
    outs = jnp.concatenate(
        [
            conv_cols.astype(jnp.bfloat16),
            back_cols.astype(jnp.bfloat16),
            taps_hi.astype(jnp.bfloat16),
            taps_lo.astype(jnp.bfloat16),
        ],
        axis=1,
    ).reshape(dev_count, first_dev, 1, 4 * chans)
    rows = lax.all_to_all(outs, AXES, split_axis=0, concat_axis=2, tiled=True)
    rows = rows.reshape(tok_rows, 4 * chans)
    conv_out = rows[:, :chans]
    input_grad = rows[:, chans : 2 * chans]
    filter_grad = rows[:, 2 * chans : 3 * chans].astype(jnp.float32) + rows[:, 3 * chans :].astype(
        jnp.float32
    )
    return (conv_out, input_grad, filter_grad)


def solution(mesh):
    placed = (P(AXES, None), P(AXES, None), P(), P(AXES, None))
    return jax.shard_map(
        per_device,
        mesh=mesh,
        in_specs=placed,
        out_specs=(P(AXES, None), P(AXES, None), P(AXES, None)),
        check_vma=False,
    )
```

profile of v0, /device:TPU:1, one launch (start us, length us, event | category | flops | bytes accessed | tf_op | source)
XLA Modules:
  0.0 102.3 jit_solution(3189238744467558587)
XLA Ops:
  0.6 1.1 %pad_maximum_fusion.4 = bf16[512,384]{1,0:T(8,128)(2,1)S(1)} fusion(bf16[512,128]{1,0:T(8,128)(2,1)} %param.7, bf16[512,128]{1,0:T(8,128)(2,1)} %param.9, bf16[512,128]{1,0:T(8,128)(2,1)} %param.6), kind=kLoop, calls=%fused_computation.15 | loop fusion | flops 1179648 | bytes 786432 | tf_op jit(solution)/shard_map/concatenate | solution.py:49
  1.7 0.3 copy.52
  2.0 23.5 %all_to_all.40 = bf16[4,128,384]{2,0,1:T(4,128)(2,1)S(1)} all-to-all(bf16[4,128,384]{2,0,1:T(4,128)(2,1)S(1)} %copy.52), channel_id=1, replica_groups=mesh['seq'=32,'dp'=4] {'seq','dp'}, dimensions={1} | all-to-all | bytes 786432 | tf_op jit(solution)/shard_map/all_to_all | solution.py:51
  25.6 1.0 fusion.24
  26.6 0.5 reshape.132
  27.1 1.1 %copy.54 = f32[2,128,2,384]{3,2,0,1:T(2,128)} copy(f32[2,128,2,384]{3,2,1,0:T(2,128)S(1)} %reshape.132) | data formatting | bytes 1572864 | tf_op jit(solution)/shard_map/reshape | solution.py:55
  28.3 4.4 %all-to-all-start.1 = ((f32[2,128,2,384]{3,2,0,1:T(2,128)}), f32[2,128,2,384]{3,2,0,1:T(2,128)S(1)}, u32[]{:S(2)}, u32[]{:S(2)}) async-start(f32[2,128,2,384]{3,2,0,1:T(2,128)} %copy.54), calls=%async_computation.1 | async-start | bytes 1572864 | tf_op jit(solution)/shard_map/all_to_all | solution.py:56
  32.9 16.1 %all-to-all-done.1 = f32[2,128,2,384]{3,2,0,1:T(2,128)S(1)} async-done(((f32[2,128,2,384]{3,2,0,1:T(2,128)}), f32[2,128,2,384]{3,2,0,1:T(2,128)S(1)}, u32[]{:S(2)}, u32[]{:S(2)}) %all-to-all-start.1) | async-done | bytes 786464 | tf_op jit(solution)/shard_map/all_to_all | solution.py:56
  49.0 0.3 fusion.22
  49.2 0.2 copy.71
  49.4 0.2 copy.70
  50.0 0.9 copy.57
  51.0 1.3 %fusion.3 = f32[256,1152]{1,0:T(8,128)S(1)} fusion(f32[256,256]{1,0:T(8,128)S(1)} %copy-done, f32[144,8,2,128]{3,2,1,0:T(2,128)S(1)} %bitcast.66), kind=kOutput, calls=%fused_computation.3 | convolution fusion | flops 905969664 | bytes 2621440 | tf_op jit(solution)/shard_map/dot_general | solution.py:76
  52.3 0.2 copy.58
  52.6 0.2 copy.59
  53.2 0.9 copy.60
  54.1 2.2 %fusion = f32[256,1152]{1,0:T(8,128)S(1)} fusion(f32[256,256]{1,0:T(8,128)S(1)} %copy-done, f32[144,8,2,128]{3,2,1,0:T(2,128)S(1)} %bitcast.65), kind=kOutput, calls=%fused_computation | convolution fusion | flops 905969664 | bytes 2621440 | tf_op jit(solution)/shard_map/dot_general | solution.py:93
  56.4 0.2 copy.61
  56.6 0.2 copy.62
  57.2 1.2 %copy.63 = f32[2,128,2,384]{3,2,0,1:T(2,128)} copy(f32[2,128,2,384]{1,3,2,0:T(8,128)S(1)} %pad_maximum_fusion.2) | data formatting | bytes 1572864 | tf_op jit(solution)/shard_map/stack | solution.py:103
  58.4 4.8 %all-to-all-start.2 = ((f32[2,128,2,384]{3,2,0,1:T(2,128)}), f32[2,128,2,384]{3,2,0,1:T(2,128)S(1)}, u32[]{:S(2)}, u32[]{:S(2)}) async-start(f32[2,128,2,384]{3,2,0,1:T(2,128)} %copy.63), calls=%async_computation.2 | async-start | bytes 1572864 | tf_op jit(solution)/shard_map/all_to_all | solution.py:104
  63.4 0.3 reshape.142
  63.7 0.1 copy.72
  64.0 15.6 %all-to-all-done.2 = f32[2,128,2,384]{3,2,0,1:T(2,128)S(1)} async-done(((f32[2,128,2,384]{3,2,0,1:T(2,128)}), f32[2,128,2,384]{3,2,0,1:T(2,128)S(1)}, u32[]{:S(2)}, u32[]{:S(2)}) %all-to-all-start.2) | async-done | bytes 786464 | tf_op jit(solution)/shard_map/all_to_all | solution.py:104
  79.6 0.3 copy.64
  79.9 0.5 reshape.135
  80.4 0.7 copy-done.1
  81.1 1.5 %fusion.25 = f32[512,384]{0,1:T(8,128)S(1)} fusion(f32[512,512]{1,0:T(8,128)S(1)} %copy-done.1, f32[512,384]{1,0:T(8,128)S(1)} %reshape.135), kind=kOutput, calls=%fused_computation.64 | convolution fusion | flops 1207959552 | bytes 2621440 | tf_op jit(solution)/shard_map/dot_general | solution.py:106
  82.8 0.2 copy.67
  83.1 17.6 %all_to_all.41 = bf16[128,4,1,512]{3,1,2,0:T(4,128)(2,1)S(1)} all-to-all(bf16[128,4,1,512]{3,1,2,0:T(4,128)(2,1)S(1)} %bitcast.74), channel_id=1, replica_groups=mesh['seq'=32,'dp'=4] {'seq','dp'}, dimensions={0} | all-to-all | bytes 1048576 | tf_op jit(solution)/shard_map/all_to_all | solution.py:121
  100.8 0.7 fusion.23
  101.6 0.7 convert_add_fusion
  (38 shorter events, 2.1 us)
Async XLA Ops:
  1.7 23.9 %copy-start.2 = (f32[512,512]{1,0:T(8,128)S(1)}, f32[512,512]{1,0:T(8,128)}, u32[]{:S(2)}) copy-start(f32[512,512]{1,0:T(8,128)} %constant.33) | copy-start | bytes 3145732
  28.3 20.7 %all-to-all-start.1 = ((f32[2,128,2,384]{3,2,0,1:T(2,128)}), f32[2,128,2,384]{3,2,0,1:T(2,128)S(1)}, u32[]{:S(2)}, u32[]{:S(2)}) async-start(f32[2,128,2,384]{3,2,0,1:T(2,128)} %copy.54), calls=%async_computation.1 | async-start | bytes 1572864 | tf_op jit(solution)/shard_map/all_to_all | solution.py:56
  50.0 1.0 copy-start
  58.4 21.2 %all-to-all-start.2 = ((f32[2,128,2,384]{3,2,0,1:T(2,128)}), f32[2,128,2,384]{3,2,0,1:T(2,128)S(1)}, u32[]{:S(2)}, u32[]{:S(2)}) async-start(f32[2,128,2,384]{3,2,0,1:T(2,128)} %copy.63), calls=%async_computation.2 | async-start | bytes 1572864 | tf_op jit(solution)/shard_map/all_to_all | solution.py:104
  79.9 1.2 %copy-start.1 = (f32[512,512]{1,0:T(8,128)S(1)}, f32[512,512]{1,0:T(8,128)}, u32[]{:S(2)}) copy-start(f32[512,512]{1,0:T(8,128)} %constant.29.clone) | copy-start | bytes 3145732
  81.1 1.5 %copy-start.3 = (f32[128]{0:T(128)S(1)}, f32[128]{0:T(128)}, u32[]{:S(2)}) copy-start(f32[128]{0:T(128)} %param.8) | copy-start | bytes 1540
where the time goes:
time: 103 us; the launch traced here: 102 us
  blocking collectives  41.2 us (40%)
  waiting for transfers between devices  31.7 us (31%)
  local copies, waits for them, and re-layouts  9.97 us (10%)
  starting transfers between devices  9.18 us (9%)
  matrix products  5.95 us (6%)
  other arithmetic  3.32 us (3%)
    all_to_all x1, blocking collectives, per_device(): lax.all_to_all(blocks, AXES, split_axis=1, concat_axis=0, tiled=True)  23.5 us
    all_to_all x1, blocking collectives, per_device(): rows = lax.all_to_all(outs, AXES, split_axis=0, concat_axis=2, tiled=True)  17.6 us
    all_to_all x1, waiting for transfers between devices, per_device(): got = lax.all_to_all(part, AXES, split_axis=1, concat_axis=1, tiled=True)  16.1 us
    all_to_all x1, waiting for transfers between devices, per_device(): lax.all_to_all(back_part, AXES, split_axis=1, concat_axis=1, tiled=True)  15.6 us
    all_to_all x1, starting transfers between devices, per_device(): lax.all_to_all(back_part, AXES, split_axis=1, concat_axis=1, tiled=True)  4.83 us
    all_to_all x1, starting transfers between devices, per_device(): got = lax.all_to_all(part, AXES, split_axis=1, concat_axis=1, tiled=True)  4.36 us
    dot_general x1, matrix products, per_device(): lax.dot_general(table_b, prod, (((0,), (0,)), ((), ())), precision=highest)  2.23 us
  transfers between devices with their start and end apart: 2, of which 2 were waited for; matrix products, arithmetic and copies ran while one was open for 1% of the time, Pallas kernels for 0%

commit v1 on v0

--- a/solution.py
+++ b/solution.py
@@ -53,7 +53,9 @@
     table_a = half_table(first_len)
     part = jnp.dot(table_a, columns, precision=highest)
     part = part.reshape(2, dev_count, slots, 3 * chans)
-    got = lax.all_to_all(part, AXES, split_axis=1, concat_axis=1, tiled=True)
+    got = jnp.concatenate(
+        lax.all_to_all(jnp.stack(jnp.split(part, lax.axis_size(AXES), axis=1)), AXES, 0, 0), axis=1
+    )
     z_re, z_im = (got[0], got[1])
     pos_b = jnp.arange(second_len, dtype=jnp.float32)[:, None]
     freq = (me * slots + jnp.arange(slots, dtype=jnp.int32)).astype(jnp.float32)[None, :]

time: 103 us -> 182 us (1.77)
  local copies, waits for them, and re-layouts: 9.97 us -> 85.3 us
  other arithmetic: 3.32 us -> 7.65 us
    unnamed x12 -> x142, local copies, waits for them, and re-layouts: 1.35 us -> 77.9 us
where the time goes in v1:
time: 182 us
  local copies, waits for them, and re-layouts  85.3 us (47%)
  blocking collectives  41.2 us (23%)
  waiting for transfers between devices  31.4 us (17%)
  starting transfers between devices  9.23 us (5%)
  other arithmetic  7.65 us (4%)
  matrix products  5.93 us (3%)
    unnamed x142, local copies, waits for them, and re-layouts  77.9 us
    all_to_all x1, blocking collectives, per_device(): lax.all_to_all(blocks, AXES, split_axis=1, concat_axis=0, tiled=True)  23.5 us
    all_to_all x1, blocking collectives, per_device(): rows = lax.all_to_all(outs, AXES, split_axis=0, concat_axis=2, tiled=True)  17.6 us
    all_to_all x1, waiting for transfers between devices, per_device(): lax.all_to_all(jnp.stack(jnp.split(part, lax.axis_size(AXES), axis=1)), A...  15.7 us
    all_to_all x1, waiting for transfers between devices, per_device(): lax.all_to_all(back_part, AXES, split_axis=1, concat_axis=1, tiled=True)  15.6 us
    all_to_all x1, starting transfers between devices, per_device(): lax.all_to_all(back_part, AXES, split_axis=1, concat_axis=1, tiled=True)  4.87 us
    all_to_all x1, starting transfers between devices, per_device(): lax.all_to_all(jnp.stack(jnp.split(part, lax.axis_size(AXES), axis=1)), A...  4.37 us
  transfers between devices with their start and end apart: 2, of which 2 were waited for; matrix products, arithmetic and copies ran while one was open for 1% of the time, Pallas kernels for 0%

profile of v1, /device:TPU:1, one launch (start us, length us, event | category | flops | bytes accessed | tf_op | source)
XLA Modules:
  0.0 181.7 jit_solution(5678261300418839187)
XLA Ops:
  0.6 1.1 pad_maximum_fusion.4
  2.0 23.5 %all_to_all.40 = bf16[4,128,384]{2,0,1:T(4,128)(2,1)S(1)} all-to-all(bf16[4,128,384]{2,0,1:T(4,128)(2,1)S(1)} %copy.716), channel_id=1, replica_groups=mesh['seq'=32,'dp'=4] {'seq','dp'}, dimensions={1} | all-to-all | bytes 786432 | tf_op jit(solution)/shard_map/all_to_all | solution.py:51
  25.6 1.0 fusion.16
  27.1 0.6 constant_dynamic-update-slice_fusion.127
  29.5 0.6 constant_dynamic-update-slice_fusion.123
  48.5 0.6 constant_dynamic-update-slice_fusion.91
  59.2 0.6 constant_dynamic-update-slice_fusion.73
  62.1 0.6 constant_dynamic-update-slice_fusion.68
  70.4 0.6 constant_dynamic-update-slice_fusion.54
  76.9 0.6 constant_dynamic-update-slice_fusion.43
  79.9 0.6 constant_dynamic-update-slice_fusion.38
  87.6 0.6 constant_dynamic-update-slice_fusion.25
  89.4 0.6 constant_dynamic-update-slice_fusion.22
  91.8 0.6 constant_dynamic-update-slice_fusion.18
  98.9 0.6 constant_dynamic-update-slice_fusion.6
  100.1 0.6 constant_dynamic-update-slice_fusion.4
  100.7 0.6 constant_dynamic-update-slice_fusion.3
  103.1 4.4 %all-to-all-start.1 = ((f32[128,2,1,2,384]{4,3,1,2,0:T(2,128)}), f32[128,2,1,2,384]{4,3,1,2,0:T(2,128)S(1)}, u32[]{:S(2)}, u32[]{:S(2)}) async-start(f32[128,2,1,2,384]{4,3,1,2,0:T(2,128)} %constant_dynamic-update-slice_fusion), calls=%async_computation.1 | async-start | bytes 1572864 | tf_op jit(solution)/shard_map/all_to_all | solution.py:57
  108.1 15.7 %all-to-all-done.1 = f32[128,2,1,2,384]{4,3,1,2,0:T(2,128)S(1)} async-done(((f32[128,2,1,2,384]{4,3,1,2,0:T(2,128)}), f32[128,2,1,2,384]{4,3,1,2,0:T(2,128)S(1)}, u32[]{:S(2)}, u32[]{:S(2)}) %all-to-all-start.1) | async-done | bytes 786464 | tf_op jit(solution)/shard_map/all_to_all | solution.py:57
  126.4 0.8 copy-done
  127.2 1.2 fusion.17
  129.4 0.9 copy.852
  130.3 2.2 %fusion = f32[256,1152]{1,0:T(8,128)S(1)} fusion(f32[256,256]{1,0:T(8,128)S(1)} %copy-done, f32[144,8,2,128]{3,2,1,0:T(2,128)S(1)} %bitcast.838), kind=kOutput, calls=%fused_computation.1 | convolution fusion | flops 905969664 | bytes 2621440 | tf_op jit(solution)/shard_map/dot_general | solution.py:95
  134.4 1.2 broadcast_select_fusion
  136.7 1.2 copy.860
  137.8 4.9 %all-to-all-start.2 = ((f32[2,128,2,384]{3,2,0,1:T(2,128)}), f32[2,128,2,384]{3,2,0,1:T(2,128)S(1)}, u32[]{:S(2)}, u32[]{:S(2)}) async-start(f32[2,128,2,384]{3,2,0,1:T(2,128)} %copy.860), calls=%async_computation.2 | async-start | bytes 1572864 | tf_op jit(solution)/shard_map/all_to_all | solution.py:106
  143.4 15.6 %all-to-all-done.2 = f32[2,128,2,384]{3,2,0,1:T(2,128)S(1)} async-done(((f32[2,128,2,384]{3,2,0,1:T(2,128)}), f32[2,128,2,384]{3,2,0,1:T(2,128)S(1)}, u32[]{:S(2)}, u32[]{:S(2)}) %all-to-all-start.2) | async-done | bytes 786464 | tf_op jit(solution)/shard_map/all_to_all | solution.py:106
  159.9 0.7 copy-done.1
  160.6 1.5 fusion.18
  162.6 17.6 %all_to_all.41 = bf16[128,4,1,512]{3,1,2,0:T(4,128)(2,1)S(1)} all-to-all(bf16[128,4,1,512]{3,1,2,0:T(4,128)(2,1)S(1)} %bitcast.846), channel_id=1, replica_groups=mesh['seq'=32,'dp'=4] {'seq','dp'}, dimensions={0} | all-to-all | bytes 1048576 | tf_op jit(solution)/shard_map/all_to_all | solution.py:123
  180.3 0.7 fusion.15
  181.0 0.7 convert_add_fusion
  (174 shorter events, 77.2 us)
Async XLA Ops:
  1.7 23.9 %copy-start.2 = (f32[512,512]{1,0:T(8,128)S(1)}, f32[512,512]{1,0:T(8,128)}, u32[]{:S(2)}) copy-start(f32[512,512]{1,0:T(8,128)} %constant.33) | copy-start | bytes 3145732
  103.1 20.7 %all-to-all-start.1 = ((f32[128,2,1,2,384]{4,3,1,2,0:T(2,128)}), f32[128,2,1,2,384]{4,3,1,2,0:T(2,128)S(1)}, u32[]{:S(2)}, u32[]{:S(2)}) async-start(f32[128,2,1,2,384]{4,3,1,2,0:T(2,128)} %constant_dynamic-update-slice_fusion), calls=%async_computation.1 | async-start | bytes 1572864 | tf_op jit(solution)/shard_map/all_to_all | solution.py:57
  126.3 1.0 copy-start
  137.8 21.2 %all-to-all-start.2 = ((f32[2,128,2,384]{3,2,0,1:T(2,128)}), f32[2,128,2,384]{3,2,0,1:T(2,128)S(1)}, u32[]{:S(2)}, u32[]{:S(2)}) async-start(f32[2,128,2,384]{3,2,0,1:T(2,128)} %copy.860), calls=%async_computation.2 | async-start | bytes 1572864 | tf_op jit(solution)/shard_map/all_to_all | solution.py:106
  159.3 1.2 copy-start.1
  160.6 1.5 copy-start.3
